TPU v7x, 256 devices: a whole 4x4x8 slice. The times are simulated.
256 devices in a mesh: expert: 32 (over x, z), tensor: 8 (over y, core).
Axes of the slice: x: 4, y: 4, z: 8, core: 2. Of those that a mesh axis runs over, the one named last changes fastest.
Arguments:
- attn_vals: bfloat16 [2048, 4096], P('expert', 'tensor'), may hold values from -6 to 6
- residual: bfloat16 [2048, 4096], P('expert', 'tensor'), may hold values from -6 to 6
- out_weight: bfloat16 [4096, 4096], P('tensor'), may hold values from -0.09375 to 0.09375
- norm_gain: float32 [4096], P('tensor'), may hold values from 0.5 to 1.5
- router_weight: float32 [4096, 8], P('tensor'), may hold values from -0.09375 to 0.09375
- routes: int32 [2048, 2], P('expert'), may hold values from 0 to 7, all different within a row; in each aligned block of 64 rows (0 to 63, 64 to 127, ...) at most 32 rows name the same one
- w_gate: bfloat16 [32, 4096, 2048], P('expert', None, 'tensor'), may hold values from -0.09375 to 0.09375
- w_up: bfloat16 [32, 4096, 2048], P('expert', None, 'tensor'), may hold values from -0.09375 to 0.09375
- w_down: bfloat16 [32, 2048, 4096], P('expert', 'tensor'), may hold values from -0.0625 to 0.0625
- slab_of: int32 [32], replicated, may hold values from 0 to 31, each once
- final_gain: float32 [4096], P('tensor'), may hold values from 0.5 to 1.5
- row_order: int32 [2048], replicated, may hold values from 0 to 2047, each once
Outputs:
- stream_out: bfloat16 [2048, 4096], P('expert', 'tensor')
- normed_out: bfloat16 [2048, 4096], P('expert', 'tensor')
Inputs may be any that keep to these rules, and one draw needn't show every extreme that they name: `routes`: the two experts of a row differ. In each aligned block of 64 rows (the rows of one device) no expert is named by more than 32 rows, and some block names one expert exactly 32 times. `slab_of`: A permutation. `row_order`: A permutation.
All inputs are finite; a program needn't handle non-finite values.
Results may differ from a plain program's by a relative error of at most 0.017.
Values may be sent and summed in bfloat16 or wider, within the bound.
No kernel may reach another device: no remote copies, remote signals or barrier semaphores. Data moves between devices by JAX's collectives and lax.ppermute only.
A program may use at most 128 MiB of HBM per device.

v0:
```python
import jax
import jax.numpy as jnp
from jax import lax
from jax.sharding import PartitionSpec as P

D = 4096
MOST = 32
EPS = 1e-05


def finish_slots(gate_val, up_val, down_weight):
    active = (jax.nn.silu(gate_val) * up_val).astype(jnp.bfloat16)
    partial_out = jnp.einsum("gmf,fd->gmd", active, down_weight, preferred_element_type=jnp.float32)
    summed = lax.psum_scatter(
        partial_out.astype(jnp.bfloat16), "tensor", scatter_dimension=2, tiled=True
    )
    return lax.all_to_all(summed, "expert", split_axis=0, concat_axis=0, tiled=True)


def final_norm(stream, final_gain):
    stream_f = stream.astype(jnp.float32)
    square_total = lax.psum(jnp.sum(stream_f * stream_f, axis=1), "tensor")
    factor = lax.rsqrt(square_total / D + EPS)
    return (stream_f * factor[:, None] * final_gain).astype(jnp.bfloat16)


def on_device(
    attn_vals,
    residual,
    out_weight,
    norm_gain,
    router_weight,
    routes,
    w_gate,
    w_up,
    w_down,
    slab_of,
    final_gain,
    row_order,
):
    groups = lax.axis_size("expert")
    row_count = attn_vals.shape[0]
    expert_count = router_weight.shape[1]
    slab_count = groups // expert_count
    partial_proj = jnp.dot(attn_vals, out_weight, preferred_element_type=jnp.float32)
    project = lax.psum_scatter(
        partial_proj.astype(jnp.bfloat16), "tensor", scatter_dimension=1, tiled=True
    ).astype(jnp.float32)
    stream_in = (residual.astype(jnp.float32) + project).astype(jnp.bfloat16)
    hidden_f = stream_in.astype(jnp.float32)
    scaled = hidden_f * norm_gain
    square_sum, logit_part = lax.psum(
        (
            jnp.sum(hidden_f * hidden_f, axis=1),
            jnp.dot(scaled, router_weight, precision=lax.Precision.HIGHEST),
        ),
        "tensor",
    )
    inverse_rms = lax.rsqrt(square_sum / D + EPS)
    normed_in = (scaled * inverse_rms[:, None]).astype(jnp.bfloat16)
    logits = logit_part * inverse_rms[:, None]
    expert_ids = jnp.arange(expert_count, dtype=jnp.int32)
    route_hot = (routes[:, :, None] == expert_ids[None, None, :]).astype(jnp.int32)
    chosen = jnp.sum(route_hot.astype(jnp.float32) * logits[:, None, :], axis=2)
    leading = jax.nn.sigmoid(chosen[:, 0] - chosen[:, 1])
    mixing = jnp.stack([leading, 1.0 - leading], axis=1)
    route_hits = jnp.sum(route_hot, axis=1)
    before_count = jnp.cumsum(route_hits, axis=0) - route_hits
    slot_ids = jnp.sum(route_hot * before_count[:, None, :], axis=2)
    slot_hot = (slot_ids[:, :, None] == jnp.arange(MOST, dtype=jnp.int32)[None, None, :]).astype(
        jnp.float32
    )
    placing = jnp.einsum("rke,rks->esr", route_hot.astype(jnp.float32), slot_hot).astype(
        jnp.bfloat16
    )
    target_expert = slab_of // slab_count
    send_map = jnp.take(placing, target_expert, axis=0)
    full_rows = lax.all_gather(normed_in, "tensor", axis=1, tiled=True)
    outgoing = jnp.einsum(
        "gsr,rd->gsd", send_map, full_rows, preferred_element_type=jnp.float32
    ).astype(jnp.bfloat16)
    arrived = lax.all_to_all(outgoing, "expert", split_axis=0, concat_axis=0, tiled=True)
    gate_val = jnp.einsum("gmd,df->gmf", arrived, w_gate[0], preferred_element_type=jnp.float32)
    up_val = jnp.einsum("gmd,df->gmf", arrived, w_up[0], preferred_element_type=jnp.float32)
    returned = finish_slots(gate_val, up_val, w_down[0])
    group_ids = jnp.arange(groups, dtype=jnp.int32)
    holder_hot = (slab_of[None, :] == group_ids[:, None]).astype(jnp.int32)
    holders = jnp.sum(holder_hot * group_ids[None, :], axis=1).reshape(expert_count, slab_count)
    row_holders = jnp.take(holders, routes, axis=0)
    flat_index = row_holders * MOST + slot_ids[:, :, None]
    flat_back = returned.reshape(groups * MOST, returned.shape[2])
    fetched = jnp.take(flat_back, flat_index.reshape(-1), axis=0).reshape(
        row_count, 2, slab_count, returned.shape[2]
    )
    expert_out = jnp.sum(fetched.astype(jnp.float32), axis=2)
    blended = jnp.sum(mixing[:, :, None] * expert_out, axis=1)
    stream = (hidden_f + blended).astype(jnp.bfloat16)
    positions = lax.axis_index("expert") * row_count + jnp.arange(row_count, dtype=jnp.int32)
    matches = (row_order[None, :] == positions[:, None]).astype(jnp.int32)
    source = jnp.sum(matches * jnp.arange(row_order.shape[0], dtype=jnp.int32)[None, :], axis=1)
    normed = final_norm(stream, final_gain)
    all_stream, all_normed = (
        lax.all_gather(stream, "expert", axis=0, tiled=True),
        lax.all_gather(normed, "expert", axis=0, tiled=True),
    )
    return (jnp.take(all_stream, source, axis=0), jnp.take(all_normed, source, axis=0))


def solution(mesh):
    return jax.shard_map(
        on_device,
        mesh=mesh,
        in_specs=(
            P("expert", "tensor"),
            P("expert", "tensor"),
            P("tensor", None),
            P("tensor"),
            P("tensor", None),
            P("expert", None),
            P("expert", None, "tensor"),
            P("expert", None, "tensor"),
            P("expert", "tensor", None),
            P(),
            P("tensor"),
            P(),
        ),
        out_specs=(P("expert", "tensor"), P("expert", "tensor")),
        check_vma=False,
    )
```

profile of v0, /device:TPU:8, one launch (start us, length us, event | category | flops | bytes accessed | tf_op | source)
XLA Modules:
  0.0 564.1 jit_solution(10908743373798955551)
XLA Ops:
  7.3 4.0 convolution_convert_fusion.2
  11.7 1.2 select_reduce_fusion.1
  13.0 0.4 fusion.13
  13.6 0.6 gather_fusion.1
  14.2 31.1 %reduce-scatter.3.cloned.1.call-done = bf16[64,512]{1,0:T(8,128)(2,1)} async-done(((bf16[64,4096]{1,0:T(8,128)(2,1)}), bf16[64,512]{1,0:T(8,128)(2,1)}) %reduce-scatter.3.cloned.1.call-update) | async-done | bytes 65552 | tf_op jit(solution)/shard_map/reduce_scatter | solution.py:46
  45.3 1.0 fusion.29
  46.3 0.2 fusion.24
  46.4 13.4 %all-reduce = (f32[64]{0:T(128)S(1)}, f32[64,8]{0,1:T(8,128)S(1)}) all-reduce(f32[64]{0:T(128)S(1)} %get-tuple-element.13, f32[64,8]{0,1:T(8,128)S(1)} %fusion.24), channel_id=1, replica_groups=mesh['expert'=32,'tensor'=8] {'tensor'}, use_global_device_ids=true, to_apply=%region_3.0 | all-reduce | flops 576 | bytes 4608 | tf_op jit(solution)/shard_map/psum | solution.py:52
  60.0 13.6 %all_gather.9 = bf16[64,4096]{1,0:T(8,128)(2,1)S(1)} all-gather(bf16[64,512]{1,0:T(8,128)(2,1)S(1)} %fusion.25), channel_id=1, replica_groups=mesh['expert'=32,'tensor'=8] {'tensor'}, dimensions={1}, use_global_device_ids=true | all-gather | bytes 589824 | tf_op jit(solution)/shard_map/all_gather | solution.py:78
  73.5 2.4 convolution_convert_fusion.1
  75.9 195.8 %all_to_all.10 = bf16[32,32,4096]{2,1,0:T(8,128)(2,1)S(1)} all-to-all(bf16[32,32,4096]{2,1,0:T(8,128)(2,1)S(1)} %convolution_convert_fusion.1), channel_id=1, replica_groups=mesh['expert'=32,'tensor'=8] {'expert'}, dimensions={0} | all-to-all | bytes 16777216 | tf_op jit(solution)/shard_map/all_to_all | solution.py:82
  271.7 3.2 copy-done.1
  275.0 2.3 fusion.3
  277.3 16.8 %convolution_convert_fusion = bf16[32,32,4096]{2,1,0:T(8,128)(2,1)} fusion(bf16[1,256,4096]{2,1,0:T(8,128)(2,1)S(1)} %copy-done, bf16[32,32,4096]{2,1,0:T(8,128)(2,1)} %copy-done.1, bf16[1,4096,256]{2,1,0:T(8,128)(2,1)} %param.21, f32[32,32,256]{2,1,0:T(8,128)S(1)} %fusion.3), kind=kOutput, calls=%fused_computation.5 | convolution fusion | flops 4300734464 | bytes 22020096 | tf_op jit(solution)/shard_map/gmf,fd->gmd/dot_general | solution.py:13
  294.2 50.3 %reduce-scatter.5.cloned.1.call-done = bf16[32,32,512]{2,1,0:T(8,128)(2,1)} async-done(((bf16[32,32,4096]{2,1,0:T(8,128)(2,1)}), bf16[32,32,512]{2,1,0:T(8,128)(2,1)}) %reduce-scatter.5.cloned.1.call-update) | async-done | bytes 1048592 | tf_op jit(solution)/shard_map/reduce_scatter | solution.py:14
  344.5 10.0 %all-to-all-start.1 = ((bf16[32,32,512]{2,1,0:T(8,128)(2,1)}), bf16[32,32,512]{2,1,0:T(8,128)(2,1)S(1)}, u32[]{:S(2)}, u32[]{:S(2)}) async-start(bf16[32,32,512]{2,1,0:T(8,128)(2,1)} %reduce-scatter.5.cloned.1.call-done), calls=%async_computation.3 | async-start | bytes 2097152 | tf_op jit(solution)/shard_map/all_to_all | solution.py:17
  355.1 0.6 gather_fusion
  356.4 0.2 fusion.34
  357.0 26.1 %all-to-all-done.1 = bf16[32,32,512]{2,1,0:T(8,128)(2,1)S(1)} async-done(((bf16[32,32,512]{2,1,0:T(8,128)(2,1)}), bf16[32,32,512]{2,1,0:T(8,128)(2,1)S(1)}, u32[]{:S(2)}, u32[]{:S(2)}) %all-to-all-start.1) | async-done | bytes 1048608 | tf_op jit(solution)/shard_map/all_to_all | solution.py:17
  383.2 2.6 gather_fusion.2
  385.8 1.2 gather.20
  386.9 0.9 convert_reduce_fusion
  387.9 0.4 multiply_reduce_fusion
  388.4 11.3 %psum.23 = f32[64]{0:T(128)S(1)} all-reduce(f32[64]{0:T(128)S(1)} %get-tuple-element.5), channel_id=1, replica_groups=mesh['expert'=32,'tensor'=8] {'tensor'}, use_global_device_ids=true, to_apply=%region_14.16 | all-reduce | flops 64 | bytes 512 | tf_op jit(solution)/shard_map/psum | solution.py:22
  399.7 0.7 fusion.28
  400.5 0.5 all-gather.3.cloned.1.call-update
  401.0 0.2 select_reduce_fusion
  401.3 74.9 %all-gather.5.cloned.1.call-done = bf16[2048,512]{1,0:T(8,128)(2,1)} async-done(((bf16[64,512]{1,0:T(8,128)(2,1)}), bf16[2048,512]{1,0:T(8,128)(2,1)}) %all-gather.5.cloned.1.call-update) | async-done | bytes 2097168 | tf_op jit(solution)/shard_map/all_gather | solution.py:104
  476.1 2.6 gather_fusion.4
  478.7 75.6 %all-gather.3.cloned.1.call-done = bf16[2048,512]{1,0:T(8,128)(2,1)} async-done(((bf16[64,512]{1,0:T(8,128)(2,1)}), bf16[2048,512]{1,0:T(8,128)(2,1)}) %all-gather.3.cloned.1.call-update) | async-done | bytes 2097168 | tf_op jit(solution)/shard_map/all_gather | solution.py:103
  554.3 2.6 gather_fusion.3
  556.9 0.7 broadcast_select_fusion
  (66 shorter events, 2.5 us)
Async XLA Ops:
  7.2 270.1 %copy-start = (bf16[1,256,4096]{2,1,0:T(8,128)(2,1)S(1)}, bf16[1,256,4096]{2,1,0:T(8,128)(2,1)}, u32[]{:S(2)}) copy-start(bf16[1,256,4096]{2,1,0:T(8,128)(2,1)} %param.22) | copy-start | bytes 6291460
  7.2 4.2 copy-start.7
  7.2 6.4 %copy-start.10 = (s32[32]{0:T(128)S(1)}, s32[32]{0:T(128)}, u32[]{:S(2)}) copy-start(s32[32]{0:T(128)} %param.23) | copy-start | bytes 388
  7.2 38.1 %copy-start.3 = (bf16[64,512]{1,0:T(8,128)(2,1)S(1)}, bf16[64,512]{1,0:T(8,128)(2,1)}, u32[]{:S(2)}) copy-start(bf16[64,512]{1,0:T(8,128)(2,1)} %param.15) | copy-start | bytes 196612
  7.2 39.0 %copy-start.5 = (f32[512]{0:T(512)S(1)}, f32[512]{0:T(512)}, u32[]{:S(2)}) copy-start(f32[512]{0:T(512)} %param.17) | copy-start | bytes 6148
  7.2 39.0 %copy-start.4 = (f32[512,8]{0,1:T(8,128)S(1)}, f32[512,8]{0,1:T(8,128)}, u32[]{:S(2)}) copy-start(f32[512,8]{0,1:T(8,128)} %param.18) | copy-start | bytes 49156
  7.2 38.0 %reduce-scatter.3.cloned.1.call-start = ((), (), s32[]{:S(2)}) async-start(), calls=%async_computation.4 | async-start | bytes 589824 | tf_op jit(solution)/shard_map/reduce_scatter | solution.py:46
  11.3 333.2 %reduce-scatter.5.cloned.1.call-start = ((), (), s32[]{:S(2)}) async-start(), calls=%async_computation.5 | async-start | bytes 9437184 | tf_op jit(solution)/shard_map/reduce_scatter | solution.py:14
  75.9 199.0 %copy-start.9 = (bf16[1,4096,256]{2,1,0:T(8,128)(2,1)S(1)}, bf16[1,4096,256]{2,1,0:T(8,128)(2,1)}, u32[]{:S(2)}) copy-start(bf16[1,4096,256]{2,1,0:T(8,128)(2,1)} %param.20) | copy-start | bytes 6291460
  271.7 3.2 copy-start.1
  344.5 38.7 %all-to-all-start.1 = ((bf16[32,32,512]{2,1,0:T(8,128)(2,1)}), bf16[32,32,512]{2,1,0:T(8,128)(2,1)S(1)}, u32[]{:S(2)}, u32[]{:S(2)}) async-start(bf16[32,32,512]{2,1,0:T(8,128)(2,1)} %reduce-scatter.5.cloned.1.call-done), calls=%async_computation.3 | async-start | bytes 2097152 | tf_op jit(solution)/shard_map/all_to_all | solution.py:17
  354.5 121.6 %all-gather.5.cloned.1.call-start = ((), (), s32[]{:S(2)}) async-start(), calls=%async_computation.7 | async-start | bytes 2162688 | tf_op jit(solution)/shard_map/all_gather | solution.py:104
  355.1 44.6 %copy-start.8 = (f32[512]{0:T(512)S(1)}, f32[512]{0:T(512)}, u32[]{:S(2)}) copy-start(f32[512]{0:T(512)} %param.24) | copy-start | bytes 6148
  355.8 45.3 %copy-start.6 = (s32[2048]{0:T(1024)S(1)}, s32[2048]{0:T(1024)}, u32[]{:S(2)}) copy-start(s32[2048]{0:T(1024)} %param.25) | copy-start | bytes 24580
  388.4 12.1 %copy-start.2 = (bf16[64,512]{1,0:T(8,128)(2,1)}, bf16[64,512]{1,0:T(8,128)(2,1)S(1)}, u32[]{:S(2)}) copy-start(bf16[64,512]{1,0:T(8,128)(2,1)S(1)} %get-tuple-element.6) | copy-start | bytes 196612
  400.4 153.9 %all-gather.3.cloned.1.call-start = ((), (), s32[]{:S(2)}) async-start(), calls=%async_computation.6 | async-start | bytes 2162688 | tf_op jit(solution)/shard_map/all_gather | solution.py:103
Sparse Core Ops, SparseCore 0:
  11.4 33.8 reduce-scatter.2
  294.3 50.1 reduce-scatter.4
  400.5 75.5 all-gather.4
  479.2 75.1 all-gather.2
where the time goes:
time: 565 us; the launch traced here: 564 us
  waiting for transfers between devices  259 us (46%)
  blocking collectives  234 us (41%)
  matrix products  26.2 us (5%)
  local copies, waits for them, and re-layouts  14.9 us (3%)
  between operations  14.1 us (2%)
  starting transfers between devices  10.2 us (2%)
  other arithmetic  6.14 us (1%)
    all_to_all x1, blocking collectives, on_device(): lax.all_to_all(outgoing, 'expert', split_axis=0, concat_axis=0, tiled=True)  196 us
    all_gather x1, waiting for transfers between devices, on_device(): lax.all_gather(stream, 'expert', axis=0, tiled=True)  75.6 us
    all_gather x1, waiting for transfers between devices, on_device(): lax.all_gather(normed, 'expert', axis=0, tiled=True)  74.9 us
    reduce_scatter x1, waiting for transfers between devices, finish_slots(): lax.psum_scatter(partial_out.astype(jnp.bfloat16), 'tensor', scatter_dime...  50.3 us
    reduce_scatter x1, waiting for transfers between devices, on_device(): lax.psum_scatter(partial_proj.astype(jnp.bfloat16), 'tensor', scatter_dim...  31.1 us
    all_to_all x1, waiting for transfers between devices, finish_slots(): lax.all_to_all(summed, 'expert', split_axis=0, concat_axis=0, tiled=True)  26.1 us
    dot_general x1, matrix products, finish_slots(): jnp.einsum('gmf,fd->gmd', active, down_weight, preferred_element_type=jnp...  16.8 us
    all_gather x1, blocking collectives, on_device(): full_rows = lax.all_gather(normed_in, 'tensor', axis=1, tiled=True)  13.6 us
  transfers between devices with their start and end apart: 5, of which 5 were waited for; matrix products, arithmetic and copies ran while one was open for 1% of the time, Pallas kernels for 0%

commit v1 on v0

--- a/solution.py
+++ b/solution.py
@@ -6,6 +6,13 @@
 D = 4096
 MOST = 32
 EPS = 1e-05
+
+
+def raise_knots(tile_in):
+    chunks = []
+    for _ in range(lax.psum(1, "expert")):
+        chunks.append(tile_in)
+    return jnp.concatenate(lax.all_to_all(jnp.stack(chunks), "expert", 0, 0), axis=0)
 
 
 def finish_slots(gate_val, up_val, down_weight):
@@ -101,7 +108,7 @@
     normed = final_norm(stream, final_gain)
     all_stream, all_normed = (
         lax.all_gather(stream, "expert", axis=0, tiled=True),
-        lax.all_gather(normed, "expert", axis=0, tiled=True),
+        raise_knots(normed),
     )
     return (jnp.take(all_stream, source, axis=0), jnp.take(all_normed, source, axis=0))
 

time: 565 us -> 504 us (0.89)
  waiting for transfers between devices: 259 us -> 191 us
  starting transfers between devices: 10.2 us -> 16 us
    all_gather x1 -> x0, waiting for transfers between devices: 74.9 us -> none  [on_device(): lax.all_gather(normed, 'expert', axis=0, tiled=True)]
    all_to_all x0 -> x1, waiting for transfers between devices: none -> 51.4 us  [raise_knots(): lax.all_to_all(jnp.stack(chunks), 'expert', 0, 0)]
    all_gather x1, waiting for transfers between devices: 75.6 us -> 31.2 us  [on_device(): lax.all_gather(stream, 'expert', axis=0, tiled=True)]
    all_to_all x0 -> x1, starting transfers between devices: none -> 5.86 us  [raise_knots(): lax.all_to_all(jnp.stack(chunks), 'expert', 0, 0)]
  transfers between devices with their start and end apart: 5 -> 5, of which waited for: 5 -> 5; matrix products, arithmetic and copies ran while one was open for 1% -> 2% of each run, Pallas kernels for 0% -> 0%
where the time goes in v1:
time: 504 us; the launch traced here: 503 us
  blocking collectives  234 us (46%)
  waiting for transfers between devices  191 us (38%)
  matrix products  26.2 us (5%)
  local copies, waits for them, and re-layouts  16.5 us (3%)
  starting transfers between devices  16 us (3%)
  between operations  14.1 us (3%)
  other arithmetic  5.51 us (1%)
    all_to_all x1, blocking collectives, on_device(): lax.all_to_all(outgoing, 'expert', split_axis=0, concat_axis=0, tiled=True)  196 us
    all_to_all x1, waiting for transfers between devices, raise_knots(): lax.all_to_all(jnp.stack(chunks), 'expert', 0, 0)  51.4 us
    reduce_scatter x1, waiting for transfers between devices, finish_slots(): lax.psum_scatter(partial_out.astype(jnp.bfloat16), 'tensor', scatter_dime...  50.3 us
    all_gather x1, waiting for transfers between devices, on_device(): lax.all_gather(stream, 'expert', axis=0, tiled=True)  31.2 us
    reduce_scatter x1, waiting for transfers between devices, on_device(): lax.psum_scatter(partial_proj.astype(jnp.bfloat16), 'tensor', scatter_dim...  31.1 us
    all_to_all x1, waiting for transfers between devices, finish_slots(): lax.all_to_all(summed, 'expert', split_axis=0, concat_axis=0, tiled=True)  26.2 us
    dot_general x1, matrix products, finish_slots(): jnp.einsum('gmf,fd->gmd', active, down_weight, preferred_element_type=jnp...  16.8 us
    all_gather x1, blocking collectives, on_device(): full_rows = lax.all_gather(normed_in, 'tensor', axis=1, tiled=True)  13.6 us
  transfers between devices with their start and end apart: 5, of which 5 were waited for; matrix products, arithmetic and copies ran while one was open for 2% of the time, Pallas kernels for 0%

profile of v1, /device:TPU:8, one launch (start us, length us, event | category | flops | bytes accessed | tf_op | source)
XLA Modules:
  0.0 503.3 jit_solution(18104267679460051192)
XLA Ops:
  7.3 4.0 convolution_convert_fusion.2
  11.7 1.2 select_reduce_fusion.1
  13.0 0.4 fusion.13
  13.6 0.6 gather_fusion.1
  14.2 31.1 %reduce-scatter.3.cloned.1.call-done = bf16[64,512]{1,0:T(8,128)(2,1)} async-done(((bf16[64,4096]{1,0:T(8,128)(2,1)}), bf16[64,512]{1,0:T(8,128)(2,1)}) %reduce-scatter.3.cloned.1.call-update) | async-done | bytes 65552 | tf_op jit(solution)/shard_map/reduce_scatter | solution.py:53
  45.3 1.0 fusion.29
  46.4 13.4 %all-reduce = (f32[64]{0:T(128)S(1)}, f32[64,8]{0,1:T(8,128)S(1)}) all-reduce(f32[64]{0:T(128)S(1)} %get-tuple-element.13, f32[64,8]{0,1:T(8,128)S(1)} %fusion.24), channel_id=1, replica_groups=mesh['expert'=32,'tensor'=8] {'tensor'}, use_global_device_ids=true, to_apply=%region_3.0 | all-reduce | flops 576 | bytes 4608 | tf_op jit(solution)/shard_map/psum | solution.py:59
  60.0 13.6 %all_gather.6 = bf16[64,4096]{1,0:T(8,128)(2,1)S(1)} all-gather(bf16[64,512]{1,0:T(8,128)(2,1)S(1)} %fusion.25), channel_id=1, replica_groups=mesh['expert'=32,'tensor'=8] {'tensor'}, dimensions={1}, use_global_device_ids=true | all-gather | bytes 589824 | tf_op jit(solution)/shard_map/all_gather | solution.py:85
  73.5 2.4 convolution_convert_fusion.1
  75.9 195.8 %all_to_all.15 = bf16[32,32,4096]{2,1,0:T(8,128)(2,1)S(1)} all-to-all(bf16[32,32,4096]{2,1,0:T(8,128)(2,1)S(1)} %convolution_convert_fusion.1), channel_id=1, replica_groups=mesh['expert'=32,'tensor'=8] {'expert'}, dimensions={0} | all-to-all | bytes 16777216 | tf_op jit(solution)/shard_map/all_to_all | solution.py:89
  271.7 3.2 copy-done.1
  275.0 2.3 fusion.3
  277.3 16.8 %convolution_convert_fusion = bf16[32,32,4096]{2,1,0:T(8,128)(2,1)} fusion(bf16[1,256,4096]{2,1,0:T(8,128)(2,1)S(1)} %copy-done, bf16[32,32,4096]{2,1,0:T(8,128)(2,1)} %copy-done.1, bf16[1,4096,256]{2,1,0:T(8,128)(2,1)} %param.21, f32[32,32,256]{2,1,0:T(8,128)S(1)} %fusion.3), kind=kOutput, calls=%fused_computation.5 | convolution fusion | flops 4300734464 | bytes 22020096 | tf_op jit(solution)/shard_map/gmf,fd->gmd/dot_general | solution.py:20
  294.2 50.3 %reduce-scatter.5.cloned.1.call-done = bf16[32,32,512]{2,1,0:T(8,128)(2,1)} async-done(((bf16[32,32,4096]{2,1,0:T(8,128)(2,1)}), bf16[32,32,512]{2,1,0:T(8,128)(2,1)}) %reduce-scatter.5.cloned.1.call-update) | async-done | bytes 1048592 | tf_op jit(solution)/shard_map/reduce_scatter | solution.py:21
  344.5 10.0 %all-to-all-start.1 = ((bf16[32,32,512]{2,1,0:T(8,128)(2,1)}), bf16[32,32,512]{2,1,0:T(8,128)(2,1)S(1)}, u32[]{:S(2)}, u32[]{:S(2)}) async-start(bf16[32,32,512]{2,1,0:T(8,128)(2,1)} %reduce-scatter.5.cloned.1.call-done), calls=%async_computation.3 | async-start | bytes 2097152 | tf_op jit(solution)/shard_map/all_to_all | solution.py:24
  355.1 0.6 gather_fusion
  356.4 0.2 fusion.34
  357.0 26.2 %all-to-all-done.1 = bf16[32,32,512]{2,1,0:T(8,128)(2,1)S(1)} async-done(((bf16[32,32,512]{2,1,0:T(8,128)(2,1)}), bf16[32,32,512]{2,1,0:T(8,128)(2,1)S(1)}, u32[]{:S(2)}, u32[]{:S(2)}) %all-to-all-start.1) | async-done | bytes 1048608 | tf_op jit(solution)/shard_map/all_to_all | solution.py:24
  383.2 2.6 gather_fusion.2
  385.8 1.2 gather.20
  387.0 0.9 convert_reduce_fusion
  387.9 0.4 multiply_reduce_fusion
  388.4 11.3 %psum.23 = f32[64]{0:T(128)S(1)} all-reduce(f32[64]{0:T(128)S(1)} %get-tuple-element.5), channel_id=1, replica_groups=mesh['expert'=32,'tensor'=8] {'tensor'}, use_global_device_ids=true, to_apply=%region_14.16 | all-reduce | flops 64 | bytes 512 | tf_op jit(solution)/shard_map/psum | solution.py:29
  399.8 1.6 stack.5
  401.3 5.9 %all-to-all-start.2 = ((bf16[32,64,512]{2,1,0:T(8,128)(2,1)}), bf16[32,64,512]{2,1,0:T(8,128)(2,1)}, u32[]{:S(2)}, u32[]{:S(2)}) async-start(bf16[32,64,512]{2,1,0:T(8,128)(2,1)} %stack.5), calls=%async_computation.4 | async-start | bytes 4194304 | tf_op jit(solution)/shard_map/all_to_all | solution.py:15
  407.3 0.7 all-gather.2.cloned.1.call-update
  408.0 0.2 select_reduce_fusion
  408.2 51.4 %all-to-all-done.2 = bf16[32,64,512]{2,1,0:T(8,128)(2,1)} async-done(((bf16[32,64,512]{2,1,0:T(8,128)(2,1)}), bf16[32,64,512]{2,1,0:T(8,128)(2,1)}, u32[]{:S(2)}, u32[]{:S(2)}) %all-to-all-start.2) | async-done | bytes 2097184 | tf_op jit(solution)/shard_map/all_to_all | solution.py:15
  459.6 2.6 gather_fusion.4
  462.2 31.2 %all-gather.2.cloned.1.call-done = bf16[2048,512]{1,0:T(8,128)(2,1)} async-done(((bf16[64,512]{1,0:T(8,128)(2,1)}), bf16[2048,512]{1,0:T(8,128)(2,1)}) %all-gather.2.cloned.1.call-update) | async-done | bytes 2097168 | tf_op jit(solution)/shard_map/all_gather | solution.py:110
  493.4 2.6 gather_fusion.3
  496.0 0.7 broadcast_select_fusion
  (66 shorter events, 2.7 us)
Async XLA Ops:
  7.2 270.1 %copy-start = (bf16[1,256,4096]{2,1,0:T(8,128)(2,1)S(1)}, bf16[1,256,4096]{2,1,0:T(8,128)(2,1)}, u32[]{:S(2)}) copy-start(bf16[1,256,4096]{2,1,0:T(8,128)(2,1)} %param.22) | copy-start | bytes 6291460
  7.2 4.2 copy-start.7
  7.2 6.4 %copy-start.10 = (s32[32]{0:T(128)S(1)}, s32[32]{0:T(128)}, u32[]{:S(2)}) copy-start(s32[32]{0:T(128)} %param.23) | copy-start | bytes 388
  7.2 38.1 %copy-start.3 = (bf16[64,512]{1,0:T(8,128)(2,1)S(1)}, bf16[64,512]{1,0:T(8,128)(2,1)}, u32[]{:S(2)}) copy-start(bf16[64,512]{1,0:T(8,128)(2,1)} %param.15) | copy-start | bytes 196612
  7.2 39.0 %copy-start.5 = (f32[512]{0:T(512)S(1)}, f32[512]{0:T(512)}, u32[]{:S(2)}) copy-start(f32[512]{0:T(512)} %param.17) | copy-start | bytes 6148
  7.2 39.0 %copy-start.4 = (f32[512,8]{0,1:T(8,128)S(1)}, f32[512,8]{0,1:T(8,128)}, u32[]{:S(2)}) copy-start(f32[512,8]{0,1:T(8,128)} %param.18) | copy-start | bytes 49156
  7.2 38.0 %reduce-scatter.3.cloned.1.call-start = ((), (), s32[]{:S(2)}) async-start(), calls=%async_computation.5 | async-start | bytes 589824 | tf_op jit(solution)/shard_map/reduce_scatter | solution.py:53
  11.3 333.2 %reduce-scatter.5.cloned.1.call-start = ((), (), s32[]{:S(2)}) async-start(), calls=%async_computation.6 | async-start | bytes 9437184 | tf_op jit(solution)/shard_map/reduce_scatter | solution.py:21
  75.9 199.0 %copy-start.9 = (bf16[1,4096,256]{2,1,0:T(8,128)(2,1)S(1)}, bf16[1,4096,256]{2,1,0:T(8,128)(2,1)}, u32[]{:S(2)}) copy-start(bf16[1,4096,256]{2,1,0:T(8,128)(2,1)} %param.20) | copy-start | bytes 6291460
  271.7 3.2 copy-start.1
  344.5 38.7 %all-to-all-start.1 = ((bf16[32,32,512]{2,1,0:T(8,128)(2,1)}), bf16[32,32,512]{2,1,0:T(8,128)(2,1)S(1)}, u32[]{:S(2)}, u32[]{:S(2)}) async-start(bf16[32,32,512]{2,1,0:T(8,128)(2,1)} %reduce-scatter.5.cloned.1.call-done), calls=%async_computation.3 | async-start | bytes 2097152 | tf_op jit(solution)/shard_map/all_to_all | solution.py:24
  355.1 44.6 %copy-start.8 = (f32[512]{0:T(512)S(1)}, f32[512]{0:T(512)}, u32[]{:S(2)}) copy-start(f32[512]{0:T(512)} %param.24) | copy-start | bytes 6148
  386.9 21.0 %copy-start.6 = (s32[2048]{0:T(1024)S(1)}, s32[2048]{0:T(1024)}, u32[]{:S(2)}) copy-start(s32[2048]{0:T(1024)} %param.25) | copy-start | bytes 24580
  388.4 18.9 %copy-start.2 = (bf16[64,512]{1,0:T(8,128)(2,1)}, bf16[64,512]{1,0:T(8,128)(2,1)S(1)}, u32[]{:S(2)}) copy-start(bf16[64,512]{1,0:T(8,128)(2,1)S(1)} %get-tuple-element.6) | copy-start | bytes 196612
  401.3 58.3 %all-to-all-start.2 = ((bf16[32,64,512]{2,1,0:T(8,128)(2,1)}), bf16[32,64,512]{2,1,0:T(8,128)(2,1)}, u32[]{:S(2)}, u32[]{:S(2)}) async-start(bf16[32,64,512]{2,1,0:T(8,128)(2,1)} %stack.5), calls=%async_computation.4 | async-start | bytes 4194304 | tf_op jit(solution)/shard_map/all_to_all | solution.py:15
  407.2 86.2 %all-gather.2.cloned.1.call-start = ((), (), s32[]{:S(2)}) async-start(), calls=%async_computation.7 | async-start | bytes 2162688 | tf_op jit(solution)/shard_map/all_gather | solution.py:110
Sparse Core Ops, SparseCore 0:
  11.4 33.8 reduce-scatter.2
  294.3 50.1 reduce-scatter.4
  411.2 82.2 all-gather.1
